TPU v7x, 256 devices: a whole 4x4x8 slice. The times are simulated.
256 devices in a mesh: ctx: 32 (over y, x, core), exp: 8 (over z).
Axes of the slice: x: 4, y: 4, z: 8, core: 2. Of those that a mesh axis runs over, the one named last changes fastest.
Arguments:
- ssm_input: bfloat16 [4096, 4096], P('ctx', 'exp'), may hold values from -6 to 6
- gate_input: bfloat16 [4096, 4096], P('ctx', 'exp'), may hold values from -6 to 6
- key_proj: bfloat16 [4096, 128], P('ctx'), may hold values from -4 to 4
- query_proj: bfloat16 [4096, 128], P('ctx'), may hold values from -4 to 4
- step_size: float32 [4096, 64], P('ctx', 'exp'), may hold values from 0 to 1, as said below
- decay_rate: float32 [64], P('exp'), may hold values from 0.5 to 1.5
- head_gain: float32 [4096], P('exp'), may hold values from 0.5 to 1.5
- residual: bfloat16 [4096, 4096], P('ctx', 'exp'), may hold values from -33 to 33
- ffn_gain: float32 [4096], replicated, may hold values from 0.5 to 1.5
- gate_weight: bfloat16 [8, 4096, 12288], P('exp', None, 'ctx'), may hold values from -0.09375 to 0.09375
- up_weight: bfloat16 [8, 4096, 12288], P('exp', None, 'ctx'), may hold values from -0.09375 to 0.09375
- down_weight: bfloat16 [8, 12288, 4096], P('exp', 'ctx'), may hold values from -0.0546875 to 0.0546875
- expert_ids: int32 [4096, 2], P('ctx'), may hold values from 0 to 7, all different within a row; in each aligned block of 128 rows (0 to 127, 128 to 255, ...) at most 48 rows name the same one
- route_weight: float32 [4096, 2], P('ctx'), may hold values from 0.5 to 2
Outputs:
- block_out: bfloat16 [4096, 4096], P('ctx', 'exp')
- expert_out: bfloat16 [4096, 4096], P('ctx', 'exp')
Inputs may be any that keep to these rules, and one draw needn't show every extreme that they name: `step_size`: step sizes are positive. `expert_ids`: the two experts of a token differ. In each aligned block of 128 rows (the tokens of one shard) no expert is named by more than 48 rows, and in some block one expert is named by exactly 48 rows.
All inputs are finite; a program needn't handle non-finite values.
Results may differ from a plain program's by a relative error of at most 0.022.
Values may be sent and summed in bfloat16 or wider, within the bound.
No kernel may reach another device: no remote copies, remote signals or barrier semaphores. Data moves between devices by JAX's collectives and lax.ppermute only.
A program may use at most 128 MiB of HBM per device.

v0:
```python
import jax
import jax.numpy as jnp
from jax import lax
from jax.sharding import Mesh, PartitionSpec as P

precise = lax.Precision.HIGHEST
CTX = ("chip", "core")


def local_block(ssm_piece, key_piece, query_piece, step_piece, decay_rate, head_count):
    row_count = ssm_piece.shape[0]
    head_width = ssm_piece.shape[1] // head_count
    values = ssm_piece.astype(jnp.float32).reshape(row_count, head_count, head_width)
    key_vals = key_piece.astype(jnp.float32)
    queries = query_piece.astype(jnp.float32)
    log_steps = -step_piece * decay_rate[None, :]
    running = jnp.cumsum(log_steps, axis=0)
    scores = jnp.dot(queries, key_vals.T, precision=precise)
    causal = (jnp.arange(row_count)[:, None] >= jnp.arange(row_count)[None, :])[:, :, None]
    spacing = running[:, None, :] - running[None, :, :]
    decays = jnp.where(causal, jnp.exp(jnp.where(causal, spacing, 0.0)), 0.0)
    within = jnp.einsum("tsh,ts,shp->thp", decays, scores, values, precision=precise)
    overall = running[-1]
    fading = jnp.exp(overall[None, :] - running)
    states = jnp.einsum("sh,shp,sn->hpn", fading, values, key_vals, precision=precise)
    return (within, running, overall, states)


def route_tables(expert_ids, route_weight, experts, capacity):
    matched = expert_ids[None, :, :] == experts[:, None, None]
    member = jnp.any(matched, axis=2).astype(jnp.int32)
    gate_sum = jnp.sum(jnp.where(matched, route_weight[None, :, :], 0.0), axis=2)
    slot_index = jnp.cumsum(member, axis=1) - 1
    positions = jnp.arange(capacity, dtype=jnp.int32)
    routing = (
        (slot_index[:, None, :] == positions[None, :, None]) & (member[:, None, :] > 0)
    ).astype(jnp.float32)
    return (routing, gate_sum)


def carried_state(overall, states):
    head_count, head_width, nstate = states.shape
    rows = head_count * head_width
    high = overall.astype(jnp.bfloat16)
    low = (overall - high.astype(jnp.float32)).astype(jnp.bfloat16)
    extra = jnp.zeros((8, nstate), jnp.bfloat16)
    extra = extra.at[0, :head_count].set(high).at[1, :head_count].set(low)
    packed = jnp.concatenate([states.astype(jnp.bfloat16).reshape(rows, nstate), extra], axis=0)
    everything = lax.all_gather(packed, CTX)
    shards = everything.shape[0]
    me = lax.axis_index(CTX)
    decay_all = everything[:, rows, :head_count].astype(jnp.float32) + everything[
        :, rows + 1, :head_count
    ].astype(jnp.float32)
    shard_of = jnp.arange(shards, dtype=jnp.int32)
    between = (shard_of[:, None] < shard_of[None, :]) & (shard_of[None, :] < me)
    spans = jnp.sum(jnp.where(between[:, :, None], decay_all[None, :, :], 0.0), axis=1)
    weight = jnp.where((shard_of < me)[:, None], jnp.exp(spans), 0.0)
    gathered = (
        everything[:, :rows, :].astype(jnp.float32).reshape(shards, head_count, head_width, nstate)
    )
    return jnp.sum(weight[:, :, None, None] * gathered, axis=0)


def on_device(
    ssm_input,
    gate_input,
    key_proj,
    query_proj,
    step_size,
    decay_rate,
    head_gain,
    residual,
    ffn_gain,
    gate_weight,
    up_weight,
    down_weight,
    expert_ids,
    route_weight,
):
    head_count = step_size.shape[1]
    row_count, channels = ssm_input.shape
    head_width = channels // head_count
    within, running, overall, states = local_block(
        ssm_input, key_proj, query_proj, step_size, decay_rate, head_count
    )
    before = carried_state(overall, states)
    carried = jnp.einsum(
        "th,hpn,tn->thp",
        jnp.exp(running),
        before,
        query_proj.astype(jnp.float32),
        precision=precise,
    )
    mixer_out = within + carried
    gated_out = mixer_out * jax.nn.silu(gate_input.astype(jnp.float32)).reshape(
        row_count, head_count, head_width
    )
    inv_rms = lax.rsqrt(jnp.mean(gated_out * gated_out, axis=2, keepdims=True) + 1e-05)
    normed = (gated_out * inv_rms).reshape(row_count, channels) * head_gain[None, :]
    block_out = (residual.astype(jnp.float32) + normed).astype(jnp.bfloat16)
    exp_count = lax.axis_size("exp")
    capacity = 3 * row_count // exp_count
    tables, gate_sum = route_tables(
        expert_ids, route_weight, jnp.arange(exp_count, dtype=jnp.int32), capacity
    )
    picked = jnp.einsum(
        "ekt,td->ekd", tables.astype(jnp.bfloat16), block_out, preferred_element_type=jnp.float32
    ).astype(jnp.bfloat16)
    arrived = lax.all_to_all(picked, "exp", 0, 0)
    own_rows = jnp.transpose(arrived, (1, 0, 2)).reshape(capacity, exp_count * channels)
    widened = own_rows.astype(jnp.float32)
    chosen = (
        widened
        * lax.rsqrt(jnp.mean(widened * widened, axis=1, keepdims=True) + 1e-06)
        * ffn_gain[None, :]
    ).astype(jnp.bfloat16)
    gate_here = gate_weight[0]
    up_here = up_weight[0]
    down_here = down_weight[0]
    swap = [(0, 1), (1, 0)]
    gate_other = lax.ppermute(gate_here, "core", swap)
    up_other = lax.ppermute(up_here, "core", swap)
    down_other = lax.ppermute(down_here, "core", swap)
    token_piece = lax.all_gather(chosen, "chip", axis=0, tiled=True)
    gate_both = jnp.concatenate([gate_here, gate_other], axis=1)
    up_both = jnp.concatenate([up_here, up_other], axis=1)
    down_both = jnp.concatenate([down_here, down_other], axis=0)
    gate_proj = jnp.dot(token_piece, gate_both, preferred_element_type=jnp.float32)
    up_proj = jnp.dot(token_piece, up_both, preferred_element_type=jnp.float32)
    hidden = (jax.nn.silu(gate_proj) * up_proj).astype(jnp.bfloat16)
    pair_sum = jnp.dot(hidden, down_both, preferred_element_type=jnp.float32).astype(jnp.bfloat16)
    summed = lax.psum_scatter(pair_sum, "chip", scatter_dimension=0, tiled=True)
    outgoing = jnp.transpose(summed.reshape(capacity, exp_count, channels), (1, 0, 2))
    returned = lax.all_to_all(outgoing, "exp", 0, 0)
    weights = tables * gate_sum[:, None, :]
    expert_out = jnp.einsum(
        "ekt,ekd->td", weights, returned.astype(jnp.float32), precision=precise
    ).astype(jnp.bfloat16)
    return (block_out, expert_out)


def solution(mesh):
    ctx_size, exp_size = mesh.devices.shape
    split = Mesh(mesh.devices.reshape(ctx_size // 2, 2, exp_size), ("chip", "core", "exp"))
    placed = (
        P(CTX, "exp"),
        P(CTX, "exp"),
        P(CTX, None),
        P(CTX, None),
        P(CTX, "exp"),
        P("exp"),
        P("exp"),
        P(CTX, "exp"),
        P(),
        P("exp", None, CTX),
        P("exp", None, CTX),
        P("exp", CTX, None),
        P(CTX, None),
        P(CTX, None),
    )
    return jax.shard_map(
        on_device,
        mesh=split,
        in_specs=placed,
        out_specs=(P(CTX, "exp"), P(CTX, "exp")),
        check_vma=False,
    )
```

profile of v0, /device:TPU:2, one launch (start us, length us, event | category | flops | bytes accessed | tf_op | source)
XLA Modules:
  0.0 297.9 jit_solution(14104984194117521374)
XLA Ops:
  7.2 0.8 negate_multiply_fusion
  8.4 1.0 copy.43
  9.9 0.7 pad_maximum_fusion
  10.7 1.0 convert_multiply_fusion.1
  11.9 0.7 fusion.46
  12.6 0.3 reduce_window_sum.23
  12.9 0.9 fusion.55
  13.8 50.6 %all-gather.6.cloned.1.call-done = bf16[16640,128]{1,0:T(8,128)(2,1)} async-done(((bf16[520,128]{1,0:T(8,128)(2,1)}), bf16[16640,128]{1,0:T(8,128)(2,1)}) %all-gather.6.cloned.1.call-update) | async-done | bytes 4259856 | tf_op jit(solution)/shard_map/all_gather | solution.py:49
  64.4 0.9 fusion.53
  66.0 4.4 %multiply_reduce_fusion = f32[512,128]{1,0:T(8,128)S(1)} fusion(bf16[32,520,128]{2,1,0:T(8,128)(2,1)} %bitcast.55, f32[32,512]{1,0:T(8,128)S(1)} %mul.90), kind=kLoop, calls=%fused_computation | loop fusion | flops 6225920 | bytes 4521984 | tf_op jit(solution)/shard_map/reduce_sum | solution.py:62
  70.7 0.8 multiply_reduce_fusion.1
  72.0 21.9 %all_to_all.10 = bf16[8,48,512]{2,1,0:T(8,128)(2,1)S(1)} all-to-all(bf16[8,48,512]{2,1,0:T(8,128)(2,1)S(1)} %convolution_convert_fusion.1), channel_id=1, replica_groups=mesh['chip'=16,'core'=2,'exp'=8] {'exp'}, dimensions={0} | all-to-all | bytes 786432 | tf_op jit(solution)/shard_map/all_to_all | solution.py:110
  94.2 0.9 multiply_convert_fusion.2
  95.3 0.5 collective-permute-start.1
  95.9 5.4 %collective-permute-done = bf16[4096,384]{1,0:T(8,128)(2,1)} collective-permute-done((bf16[4096,384]{1,0:T(8,128)(2,1)}, bf16[4096,384]{1,0:T(8,128)(2,1)}, u32[]{:S(2)}, u32[]{:S(2)}) %collective-permute-start) | collective-permute-done | bytes 3145760 | tf_op jit(solution)/shard_map/ppermute | solution.py:122
  101.3 54.9 %all-gather.4.cloned.1.call-done = bf16[768,4096]{1,0:T(8,128)(2,1)} async-done(((bf16[48,4096]{1,0:T(8,128)(2,1)}), bf16[768,4096]{1,0:T(8,128)(2,1)}) %all-gather.4.cloned.1.call-update) | async-done | bytes 6291472 | tf_op jit(solution)/shard_map/all_gather | solution.py:125
  156.2 9.8 %fusion = f32[768,768]{1,0:T(8,128)S(1)} fusion(bf16[768,4096]{1,0:T(8,128)(2,1)} %all-gather.4.cloned.1.call-done, bf16[4096,384]{1,0:T(8,128)(2,1)} %collective-permute-done, bf16[4096,384]{1,0:T(8,128)(2,1)} %bitcast.65), kind=kOutput, calls=%fused_computation.2 | convolution fusion | flops 4844421120 | bytes 14942208 | tf_op jit(solution)/shard_map/dot_general | solution.py:129
  166.0 7.1 %fusion.4 = f32[768,768]{1,0:T(8,128)S(1)} fusion(bf16[768,4096]{1,0:T(8,128)(2,1)S(1)} %copy-done.8, bf16[4096,384]{1,0:T(8,128)(2,1)} %collective-permute-done.1, bf16[4096,384]{1,0:T(8,128)(2,1)S(1)} %bitcast.67), kind=kOutput, calls=%fused_computation.6 | convolution fusion | flops 4844421120 | bytes 14942208 | tf_op jit(solution)/shard_map/dot_general | solution.py:130
  173.1 8.9 %convolution_convert_fusion = bf16[768,4096]{1,0:T(8,128)(2,1)} fusion(bf16[384,4096]{1,0:T(8,128)(2,1)} %collective-permute-done.2, bf16[384,4096]{1,0:T(8,128)(2,1)S(1)} %bitcast.69, f32[768,768]{1,0:T(8,128)S(1)} %fusion.4, f32[768,768]{1,0:T(8,128)S(1)} %fusion), kind=kOutput, calls=%fused_computation.1 | convolution fusion | flops 4851105792 | bytes 17301504 | tf_op jit(solution)/shard_map/dot_general | solution.py:132
  182.0 86.4 %reduce-scatter.2.cloned.1.call-done = bf16[48,4096]{1,0:T(8,128)(2,1)} async-done(((bf16[768,4096]{1,0:T(8,128)(2,1)}), bf16[48,4096]{1,0:T(8,128)(2,1)}) %reduce-scatter.2.cloned.1.call-update) | async-done | bytes 393232 | tf_op jit(solution)/shard_map/reduce_scatter | solution.py:133
  268.4 1.8 copy.57
  270.2 7.0 %all-to-all-start.1 = ((bf16[8,48,512]{2,1,0:T(8,128)(2,1)}), bf16[8,48,512]{2,1,0:T(8,128)(2,1)S(1)}, u32[]{:S(2)}, u32[]{:S(2)}) async-start(bf16[8,48,512]{2,1,0:T(8,128)(2,1)} %bitcast.53), calls=%async_computation.2 | async-start | bytes 786432 | tf_op jit(solution)/shard_map/all_to_all | solution.py:135
  277.2 13.1 %all-to-all-done.1 = bf16[8,48,512]{2,1,0:T(8,128)(2,1)S(1)} async-done(((bf16[8,48,512]{2,1,0:T(8,128)(2,1)}), bf16[8,48,512]{2,1,0:T(8,128)(2,1)S(1)}, u32[]{:S(2)}, u32[]{:S(2)}) %all-to-all-start.1) | async-done | bytes 393248 | tf_op jit(solution)/shard_map/all_to_all | solution.py:135
  290.3 1.1 fusion.15
  (67 shorter events, 3.1 us)
Async XLA Ops:
  7.2 2.3 copy-start
  7.2 63.2 %copy-start.2 = (bf16[128,128]{1,0:T(8,128)(2,1)S(1)}, bf16[128,128]{1,0:T(8,128)(2,1)}, u32[]{:S(2)}) copy-start(bf16[128,128]{1,0:T(8,128)(2,1)} %param.21) | copy-start | bytes 98308
  7.2 57.3 %all-gather.6.cloned.1.call-start = ((), (), s32[]{:S(2)}) async-start(), calls=%async_computation.5 | async-start | bytes 4392960 | tf_op jit(solution)/shard_map/all_gather | solution.py:49
  10.6 145.6 %all-gather.4.cloned.1.call-start = ((), (), s32[]{:S(2)}) async-start(), calls=%async_computation.3 | async-start | bytes 6684672 | tf_op jit(solution)/shard_map/all_gather | solution.py:125
  11.7 59.9 %copy-start.3 = (bf16[128,512]{1,0:T(8,128)(2,1)S(1)}, bf16[128,512]{1,0:T(8,128)(2,1)}, u32[]{:S(2)}) copy-start(bf16[128,512]{1,0:T(8,128)(2,1)} %param.25) | copy-start | bytes 393220
  11.7 59.9 %copy-start.6 = (f32[512]{0:T(512)S(1)}, f32[512]{0:T(512)}, u32[]{:S(2)}) copy-start(f32[512]{0:T(512)} %param.24) | copy-start | bytes 6148
  70.4 23.9 %copy-start.4 = (f32[4096]{0:T(1024)S(1)}, f32[4096]{0:T(1024)}, u32[]{:S(2)}) copy-start(f32[4096]{0:T(1024)} %param.26) | copy-start | bytes 49156
  71.7 94.2 %copy-start.1 = (bf16[128,512]{1,0:T(8,128)(2,1)}, bf16[128,512]{1,0:T(8,128)(2,1)S(1)}, u32[]{:S(2)}) copy-start(bf16[128,512]{1,0:T(8,128)(2,1)S(1)} %add_convert_fusion) | copy-start | bytes 393220
  95.2 173.2 %reduce-scatter.2.cloned.1.call-start = ((), (), s32[]{:S(2)}) async-start(), calls=%async_computation.4 | async-start | bytes 6684672 | tf_op jit(solution)/shard_map/reduce_scatter | solution.py:133
  95.2 6.1 %collective-permute-start = (bf16[4096,384]{1,0:T(8,128)(2,1)}, bf16[4096,384]{1,0:T(8,128)(2,1)}, u32[]{:S(2)}, u32[]{:S(2)}) collective-permute-start(bf16[4096,384]{1,0:T(8,128)(2,1)} %bitcast.64), channel_id=1, source_target_pairs={{0,8},{8,0},{1,9},{9,1},{2,10},{10,2},{3,11},{11,3},{4,12},{12,4},... | collective-permute-start | bytes 9437192 | tf_op jit(solution)/shard_map/ppermute | solution.py:122
  95.3 70.7 %collective-permute-start.1 = (bf16[4096,384]{1,0:T(8,128)(2,1)}, bf16[4096,384]{1,0:T(8,128)(2,1)}, u32[]{:S(2)}, u32[]{:S(2)}) collective-permute-start(bf16[4096,384]{1,0:T(8,128)(2,1)} %bitcast.66), channel_id=1, source_target_pairs={{0,8},{8,0},{1,9},{9,1},{2,10},{10,2},{3,11},{11,3},{4,12},{12,4},... | collective-permute-start | bytes 9437192 | tf_op jit(solution)/shard_map/ppermute | solution.py:123
  95.8 70.2 %copy-start.9 = (bf16[1,4096,384]{2,1,0:T(8,128)(2,1)S(1)}, bf16[1,4096,384]{2,1,0:T(8,128)(2,1)}, u32[]{:S(2)}) copy-start(bf16[1,4096,384]{2,1,0:T(8,128)(2,1)} %param.28) | copy-start | bytes 9437188
  95.8 77.3 %collective-permute-start.2 = (bf16[384,4096]{1,0:T(8,128)(2,1)}, bf16[384,4096]{1,0:T(8,128)(2,1)}, u32[]{:S(2)}, u32[]{:S(2)}) collective-permute-start(bf16[384,4096]{1,0:T(8,128)(2,1)} %bitcast.68), channel_id=1, source_target_pairs={{0,8},{8,0},{1,9},{9,1},{2,10},{10,2},{3,11},{11,3},{4,12},{12,4},... | collective-permute-start | bytes 9437192 | tf_op jit(solution)/shard_map/ppermute | solution.py:124
  156.2 9.8 %copy-start.8 = (bf16[768,4096]{1,0:T(8,128)(2,1)S(1)}, bf16[768,4096]{1,0:T(8,128)(2,1)}, u32[]{:S(2)}) copy-start(bf16[768,4096]{1,0:T(8,128)(2,1)} %all-gather.4.cloned.1.call-done) | copy-start | bytes 18874372
  166.0 7.2 %copy-start.10 = (bf16[1,384,4096]{2,1,0:T(8,128)(2,1)S(1)}, bf16[1,384,4096]{2,1,0:T(8,128)(2,1)}, u32[]{:S(2)}) copy-start(bf16[1,384,4096]{2,1,0:T(8,128)(2,1)} %param.29) | copy-start | bytes 9437188
  182.0 95.2 %copy-start.5 = (s32[128,2]{0,1:T(2,128)S(1)}, s32[128,2]{0,1:T(2,128)}, u32[]{:S(2)}) copy-start(s32[128,2]{0,1:T(2,128)} %param.30) | copy-start | bytes 3076
  182.0 95.2 %copy-start.7 = (f32[128,2]{0,1:T(2,128)S(1)}, f32[128,2]{0,1:T(2,128)}, u32[]{:S(2)}) copy-start(f32[128,2]{0,1:T(2,128)} %param.31) | copy-start | bytes 3076
  270.2 20.1 %all-to-all-start.1 = ((bf16[8,48,512]{2,1,0:T(8,128)(2,1)}), bf16[8,48,512]{2,1,0:T(8,128)(2,1)S(1)}, u32[]{:S(2)}, u32[]{:S(2)}) async-start(bf16[8,48,512]{2,1,0:T(8,128)(2,1)} %bitcast.53), calls=%async_computation.2 | async-start | bytes 786432 | tf_op jit(solution)/shard_map/all_to_all | solution.py:135
Sparse Core Ops, SparseCore 0:
  10.7 53.7 all-gather.5
  95.3 60.8 all-gather.3
  182.2 86.1 reduce-scatter.1
where the time goes:
time: 298 us
  waiting for transfers between devices  210 us (70%)
  matrix products  29.3 us (10%)
  blocking collectives  21.9 us (7%)
  between operations  14.1 us (5%)
  other arithmetic  9.51 us (3%)
  starting transfers between devices  7.8 us (3%)
  local copies, waits for them, and re-layouts  4.92 us (2%)
    reduce_scatter x1, waiting for transfers between devices, on_device(): summed = lax.psum_scatter(pair_sum, 'chip', scatter_dimension=0, tiled=True)  86.4 us
    all_gather x1, waiting for transfers between devices, on_device(): token_piece = lax.all_gather(chosen, 'chip', axis=0, tiled=True)  54.9 us
    all_gather x1, waiting for transfers between devices, carried_state(): everything = lax.all_gather(packed, CTX)  50.6 us
    all_to_all x1, blocking collectives, on_device(): arrived = lax.all_to_all(picked, 'exp', 0, 0)  21.9 us
    all_to_all x1, waiting for transfers between devices, on_device(): returned = lax.all_to_all(outgoing, 'exp', 0, 0)  13.1 us
    dot_general x1, matrix products, on_device(): jnp.dot(token_piece, gate_both, preferred_element_type=jnp.float32)  9.77 us
    dot_general x1, matrix products, on_device(): jnp.dot(hidden, down_both, preferred_element_type=jnp.float32)  8.86 us
    dot_general x1, matrix products, on_device(): up_proj = jnp.dot(token_piece, up_both, preferred_element_type=jnp.float32)  7.1 us
  transfers between devices with their start and end apart: 7, of which 5 were waited for; matrix products, arithmetic and copies ran while one was open for 7% of the time, Pallas kernels for 0%

commit v1 on v0

--- a/solution.py
+++ b/solution.py
@@ -122,7 +122,10 @@
     gate_other = lax.ppermute(gate_here, "core", swap)
     up_other = lax.ppermute(up_here, "core", swap)
     down_other = lax.ppermute(down_here, "core", swap)
-    token_piece = lax.all_gather(chosen, "chip", axis=0, tiled=True)
+    n_dev = lax.axis_size("chip")
+    blocks = jnp.stack([chosen for _ in range(n_dev)])
+    blocks = lax.all_to_all(blocks, "chip", split_axis=0, concat_axis=0)
+    token_piece = jnp.concatenate(blocks, axis=0)
     gate_both = jnp.concatenate([gate_here, gate_other], axis=1)
     up_both = jnp.concatenate([up_here, up_other], axis=1)
     down_both = jnp.concatenate([down_here, down_other], axis=0)

time: 298 us -> 335 us (1.12)
  waiting for transfers between devices: 210 us -> 237 us
  starting transfers between devices: 7.8 us -> 13.8 us
  local copies, waits for them, and re-layouts: 4.92 us -> 8.36 us
    all_to_all x0 -> x1, waiting for transfers between devices: none -> 82.5 us  [on_device(): blocks = lax.all_to_all(blocks, 'chip', split_axis=0, concat_axis=0)]
    all_gather x1 -> x0, waiting for transfers between devices: 54.9 us -> none  [on_device(): token_piece = lax.all_gather(chosen, 'chip', axis=0, tiled=True)]
    all_to_all x0 -> x1, starting transfers between devices: none -> 6.01 us  [on_device(): blocks = lax.all_to_all(blocks, 'chip', split_axis=0, concat_axis=0)]
    another operation x0 -> x1, local copies, waits for them, and re-layouts: none -> 3.44 us  [on_device(): blocks = jnp.stack([chosen for _ in range(n_dev)])]
  transfers between devices with their start and end apart: 7 -> 7, of which waited for: 5 -> 5; matrix products, arithmetic and copies ran while one was open for 7% -> 6% of each run, Pallas kernels for 0% -> 0%
where the time goes in v1:
time: 335 us; the launch traced here: 334 us
  waiting for transfers between devices  237 us (71%)
  matrix products  30.3 us (9%)
  blocking collectives  21.9 us (7%)
  between operations  14.4 us (4%)
  starting transfers between devices  13.8 us (4%)
  other arithmetic  8.76 us (3%)
  local copies, waits for them, and re-layouts  8.36 us (2%)
    reduce_scatter x1, waiting for transfers between devices, on_device(): summed = lax.psum_scatter(pair_sum, 'chip', scatter_dimension=0, tiled=True)  85.2 us
    all_to_all x1, waiting for transfers between devices, on_device(): blocks = lax.all_to_all(blocks, 'chip', split_axis=0, concat_axis=0)  82.5 us
    all_gather x1, waiting for transfers between devices, carried_state(): everything = lax.all_gather(packed, CTX)  50.7 us
    all_to_all x1, blocking collectives, on_device(): arrived = lax.all_to_all(picked, 'exp', 0, 0)  21.9 us
    all_to_all x1, waiting for transfers between devices, on_device(): returned = lax.all_to_all(outgoing, 'exp', 0, 0)  13 us
    dot_general x1, matrix products, on_device(): jnp.dot(hidden, down_both, preferred_element_type=jnp.float32)  8.94 us
    dot_general x1, matrix products, on_device(): up_proj = jnp.dot(token_piece, up_both, preferred_element_type=jnp.float32)  8.92 us
    dot_general x1, matrix products, on_device(): jnp.dot(token_piece, gate_both, preferred_element_type=jnp.float32)  8.92 us
  transfers between devices with their start and end apart: 7, of which 5 were waited for; matrix products, arithmetic and copies ran while one was open for 6% of the time, Pallas kernels for 0%

profile of v1, /device:TPU:2, one launch (start us, length us, event | category | flops | bytes accessed | tf_op | source)
XLA Modules:
  0.0 334.2 jit_solution(14264616988498677255)
XLA Ops:
  7.2 0.8 negate_multiply_fusion
  8.4 1.0 copy.43
  9.9 0.7 pad_maximum_fusion
  10.7 1.0 convert_multiply_fusion.1
  11.8 0.7 fusion.46
  12.9 0.9 fusion.55
  13.8 50.7 %all-gather.3.cloned.1.call-done = bf16[16640,128]{1,0:T(8,128)(2,1)} async-done(((bf16[520,128]{1,0:T(8,128)(2,1)}), bf16[16640,128]{1,0:T(8,128)(2,1)}) %all-gather.3.cloned.1.call-update) | async-done | bytes 4259856 | tf_op jit(solution)/shard_map/all_gather | solution.py:49
  64.4 0.9 fusion.53
  66.0 4.4 %multiply_reduce_fusion = f32[512,128]{1,0:T(8,128)S(1)} fusion(bf16[32,520,128]{2,1,0:T(8,128)(2,1)} %bitcast.56, f32[32,512]{1,0:T(8,128)S(1)} %mul.94), kind=kLoop, calls=%fused_computation | loop fusion | flops 6225920 | bytes 4521984 | tf_op jit(solution)/shard_map/reduce_sum | solution.py:62
  70.7 0.8 multiply_reduce_fusion.1
  72.0 21.9 %all_to_all.15 = bf16[8,48,512]{2,1,0:T(8,128)(2,1)S(1)} all-to-all(bf16[8,48,512]{2,1,0:T(8,128)(2,1)S(1)} %convolution_convert_fusion.1), channel_id=1, replica_groups=mesh['chip'=16,'core'=2,'exp'=8] {'exp'}, dimensions={0} | all-to-all | bytes 786432 | tf_op jit(solution)/shard_map/all_to_all | solution.py:110
  94.4 3.4 %stack.2 = bf16[16,48,4096]{2,1,0:T(8,128)(2,1)} broadcast(bf16[48,4096]{1,0:T(8,128)(2,1)S(1)} %multiply_convert_fusion.2), dimensions={1,2} | broadcast | bytes 6684672 | tf_op jit(solution)/shard_map/stack | solution.py:126
  97.8 6.0 %all-to-all-start.1 = ((bf16[16,48,4096]{2,1,0:T(8,128)(2,1)}), bf16[16,48,4096]{2,1,0:T(8,128)(2,1)}, u32[]{:S(2)}, u32[]{:S(2)}) async-start(bf16[16,48,4096]{2,1,0:T(8,128)(2,1)} %stack.2), calls=%async_computation.1 | async-start | bytes 12582912 | tf_op jit(solution)/shard_map/all_to_all | solution.py:127
  104.0 0.5 collective-permute-start.1
  104.6 5.2 %collective-permute-done = bf16[4096,384]{1,0:T(8,128)(2,1)} collective-permute-done((bf16[4096,384]{1,0:T(8,128)(2,1)S(1)}, bf16[4096,384]{1,0:T(8,128)(2,1)}, u32[]{:S(2)}, u32[]{:S(2)}) %collective-permute-start) | collective-permute-done | bytes 3145760 | tf_op jit(solution)/shard_map/ppermute | solution.py:122
  109.8 82.5 %all-to-all-done.1 = bf16[16,48,4096]{2,1,0:T(8,128)(2,1)} async-done(((bf16[16,48,4096]{2,1,0:T(8,128)(2,1)}), bf16[16,48,4096]{2,1,0:T(8,128)(2,1)}, u32[]{:S(2)}, u32[]{:S(2)}) %all-to-all-start.1) | async-done | bytes 6291488 | tf_op jit(solution)/shard_map/all_to_all | solution.py:127
  192.3 8.9 %fusion = f32[768,768]{1,0:T(8,128)S(1)} fusion(bf16[768,4096]{1,0:T(8,128)(2,1)} %bitcast.14, bf16[4096,384]{1,0:T(8,128)(2,1)} %collective-permute-done, bf16[4096,384]{1,0:T(8,128)(2,1)S(1)} %bitcast.66), kind=kOutput, calls=%fused_computation.2 | convolution fusion | flops 4844421120 | bytes 14942208 | tf_op jit(solution)/shard_map/dot_general | solution.py:132
  201.2 8.9 %fusion.4 = f32[768,768]{1,0:T(8,128)S(1)} fusion(bf16[768,4096]{1,0:T(8,128)(2,1)} %bitcast.14, bf16[4096,384]{1,0:T(8,128)(2,1)} %collective-permute-done.1, bf16[4096,384]{1,0:T(8,128)(2,1)S(1)} %bitcast.68), kind=kOutput, calls=%fused_computation.6 | convolution fusion | flops 4844421120 | bytes 14942208 | tf_op jit(solution)/shard_map/dot_general | solution.py:133
  210.2 8.9 %convolution_convert_fusion = bf16[768,4096]{1,0:T(8,128)(2,1)} fusion(bf16[384,4096]{1,0:T(8,128)(2,1)} %collective-permute-done.2, bf16[384,4096]{1,0:T(8,128)(2,1)S(1)} %bitcast.70, f32[768,768]{1,0:T(8,128)S(1)} %fusion.4, f32[768,768]{1,0:T(8,128)S(1)} %fusion), kind=kOutput, calls=%fused_computation.1 | convolution fusion | flops 4851105792 | bytes 17301504 | tf_op jit(solution)/shard_map/dot_general | solution.py:135
  219.2 85.2 %reduce-scatter.2.cloned.1.call-done = bf16[48,4096]{1,0:T(8,128)(2,1)} async-done(((bf16[768,4096]{1,0:T(8,128)(2,1)}), bf16[48,4096]{1,0:T(8,128)(2,1)}) %reduce-scatter.2.cloned.1.call-update) | async-done | bytes 393232 | tf_op jit(solution)/shard_map/reduce_scatter | solution.py:136
  304.4 1.8 copy.57
  306.2 7.0 %all-to-all-start.2 = ((bf16[8,48,512]{2,1,0:T(8,128)(2,1)}), bf16[8,48,512]{2,1,0:T(8,128)(2,1)S(1)}, u32[]{:S(2)}, u32[]{:S(2)}) async-start(bf16[8,48,512]{2,1,0:T(8,128)(2,1)} %bitcast.54), calls=%async_computation.3 | async-start | bytes 786432 | tf_op jit(solution)/shard_map/all_to_all | solution.py:138
  313.2 13.0 %all-to-all-done.2 = bf16[8,48,512]{2,1,0:T(8,128)(2,1)S(1)} async-done(((bf16[8,48,512]{2,1,0:T(8,128)(2,1)}), bf16[8,48,512]{2,1,0:T(8,128)(2,1)S(1)}, u32[]{:S(2)}, u32[]{:S(2)}) %all-to-all-start.2) | async-done | bytes 393248 | tf_op jit(solution)/shard_map/all_to_all | solution.py:138
  326.3 1.1 fusion.15
  (67 shorter events, 3.5 us)
Async XLA Ops:
  7.2 2.3 copy-start
  7.2 63.2 %copy-start.2 = (bf16[128,128]{1,0:T(8,128)(2,1)S(1)}, bf16[128,128]{1,0:T(8,128)(2,1)}, u32[]{:S(2)}) copy-start(bf16[128,128]{1,0:T(8,128)(2,1)} %param.21) | copy-start | bytes 98308
  7.2 57.3 %all-gather.3.cloned.1.call-start = ((), (), s32[]{:S(2)}) async-start(), calls=%async_computation.5 | async-start | bytes 4392960 | tf_op jit(solution)/shard_map/all_gather | solution.py:49
  11.7 60.0 %copy-start.3 = (bf16[128,512]{1,0:T(8,128)(2,1)S(1)}, bf16[128,512]{1,0:T(8,128)(2,1)}, u32[]{:S(2)}) copy-start(bf16[128,512]{1,0:T(8,128)(2,1)} %param.25) | copy-start | bytes 393220
  11.7 60.0 %copy-start.6 = (f32[512]{0:T(512)S(1)}, f32[512]{0:T(512)}, u32[]{:S(2)}) copy-start(f32[512]{0:T(512)} %param.24) | copy-start | bytes 6148
  70.4 23.9 %copy-start.4 = (f32[4096]{0:T(1024)S(1)}, f32[4096]{0:T(1024)}, u32[]{:S(2)}) copy-start(f32[4096]{0:T(1024)} %param.26) | copy-start | bytes 49156
  71.7 26.1 %copy-start.1 = (bf16[128,512]{1,0:T(8,128)(2,1)}, bf16[128,512]{1,0:T(8,128)(2,1)S(1)}, u32[]{:S(2)}) copy-start(bf16[128,512]{1,0:T(8,128)(2,1)S(1)} %add_convert_fusion) | copy-start | bytes 393220
  97.8 6.1 %copy-start.8 = (bf16[1,4096,384]{2,1,0:T(8,128)(2,1)S(1)}, bf16[1,4096,384]{2,1,0:T(8,128)(2,1)}, u32[]{:S(2)}) copy-start(bf16[1,4096,384]{2,1,0:T(8,128)(2,1)} %param.27) | copy-start | bytes 9437188
  97.8 94.5 %all-to-all-start.1 = ((bf16[16,48,4096]{2,1,0:T(8,128)(2,1)}), bf16[16,48,4096]{2,1,0:T(8,128)(2,1)}, u32[]{:S(2)}, u32[]{:S(2)}) async-start(bf16[16,48,4096]{2,1,0:T(8,128)(2,1)} %stack.2), calls=%async_computation.1 | async-start | bytes 12582912 | tf_op jit(solution)/shard_map/all_to_all | solution.py:127
  103.8 200.5 %reduce-scatter.2.cloned.1.call-start = ((), (), s32[]{:S(2)}) async-start(), calls=%async_computation.4 | async-start | bytes 6684672 | tf_op jit(solution)/shard_map/reduce_scatter | solution.py:136
  103.9 5.9 %collective-permute-start = (bf16[4096,384]{1,0:T(8,128)(2,1)S(1)}, bf16[4096,384]{1,0:T(8,128)(2,1)}, u32[]{:S(2)}, u32[]{:S(2)}) collective-permute-start(bf16[4096,384]{1,0:T(8,128)(2,1)S(1)} %bitcast.65), channel_id=1, source_target_pairs={{0,8},{8,0},{1,9},{9,1},{2,10},{10,2},{3,11},{11,3},{4,12},{12,4},... | collective-permute-start | bytes 9437192 | tf_op jit(solution)/shard_map/ppermute | solution.py:122
  104.0 97.2 %collective-permute-start.1 = (bf16[4096,384]{1,0:T(8,128)(2,1)}, bf16[4096,384]{1,0:T(8,128)(2,1)}, u32[]{:S(2)}, u32[]{:S(2)}) collective-permute-start(bf16[4096,384]{1,0:T(8,128)(2,1)} %bitcast.67), channel_id=1, source_target_pairs={{0,8},{8,0},{1,9},{9,1},{2,10},{10,2},{3,11},{11,3},{4,12},{12,4},... | collective-permute-start | bytes 9437192 | tf_op jit(solution)/shard_map/ppermute | solution.py:123
  104.5 105.7 %collective-permute-start.2 = (bf16[384,4096]{1,0:T(8,128)(2,1)}, bf16[384,4096]{1,0:T(8,128)(2,1)}, u32[]{:S(2)}, u32[]{:S(2)}) collective-permute-start(bf16[384,4096]{1,0:T(8,128)(2,1)} %bitcast.69), channel_id=1, source_target_pairs={{0,8},{8,0},{1,9},{9,1},{2,10},{10,2},{3,11},{11,3},{4,12},{12,4},... | collective-permute-start | bytes 9437192 | tf_op jit(solution)/shard_map/ppermute | solution.py:124
  192.3 9.0 %copy-start.9 = (bf16[1,4096,384]{2,1,0:T(8,128)(2,1)S(1)}, bf16[1,4096,384]{2,1,0:T(8,128)(2,1)}, u32[]{:S(2)}) copy-start(bf16[1,4096,384]{2,1,0:T(8,128)(2,1)} %param.28) | copy-start | bytes 9437188
  201.2 9.0 %copy-start.10 = (bf16[1,384,4096]{2,1,0:T(8,128)(2,1)S(1)}, bf16[1,384,4096]{2,1,0:T(8,128)(2,1)}, u32[]{:S(2)}) copy-start(bf16[1,384,4096]{2,1,0:T(8,128)(2,1)} %param.29) | copy-start | bytes 9437188
  219.1 94.0 %copy-start.5 = (s32[128,2]{0,1:T(2,128)S(1)}, s32[128,2]{0,1:T(2,128)}, u32[]{:S(2)}) copy-start(s32[128,2]{0,1:T(2,128)} %param.30) | copy-start | bytes 3076
  219.1 94.0 %copy-start.7 = (f32[128,2]{0,1:T(2,128)S(1)}, f32[128,2]{0,1:T(2,128)}, u32[]{:S(2)}) copy-start(f32[128,2]{0,1:T(2,128)} %param.31) | copy-start | bytes 3076
  306.2 20.1 %all-to-all-start.2 = ((bf16[8,48,512]{2,1,0:T(8,128)(2,1)}), bf16[8,48,512]{2,1,0:T(8,128)(2,1)S(1)}, u32[]{:S(2)}, u32[]{:S(2)}) async-start(bf16[8,48,512]{2,1,0:T(8,128)(2,1)} %bitcast.54), calls=%async_computation.3 | async-start | bytes 786432 | tf_op jit(solution)/shard_map/all_to_all | solution.py:138
Sparse Core Ops, SparseCore 0:
  10.7 53.7 all-gather.2
  219.3 85.0 reduce-scatter.1
